TPU v7x, 256 devices: a whole 4x4x8 slice. The times are simulated.
256 devices in a mesh: blk: 32 (over z, y_lo, core), grp: 8 (over x, y_hi).
Axes of the slice: x: 4, y: 4 (y_hi: 2, y_lo: 2; y = y_hi * 2 + y_lo), z: 8, core: 2. Of those that a mesh axis runs over, the one named last changes fastest.
Arguments:
- low_sites: float32 [8, 32768], P(None, ('blk', 'grp')), may hold values from -6 to 6
- low_probes: float32 [8, 32768], P(None, ('blk', 'grp')), may hold values from -0.03314563 to 0.03314563
- high_probes: float32 [8, 16384], P(None, ('blk', 'grp')), may hold values from -0.03314563 to 0.03314563
- nested: int32 [16384], P(('blk', 'grp')), may hold values from 0 to 32767, as said below
- inv_len_low: float32 [8], replicated, may hold values from 0.15 to 0.6
- inv_len_diff: float32 [8], replicated, may hold values from 0.2 to 0.8
Outputs:
- low_out: float32 [8, 32768], P(None, ('blk', 'grp'))
- high_out: float32 [8, 16384], P(None, ('blk', 'grp'))
Inputs may be any that keep to these rules, and one draw needn't show every extreme that they name: `nested`: entries are distinct; the high sites in the aligned block of 512 entries number b all lie among the low sites b * 1024 to (b + 1) * 1024 - 1.
All inputs are finite; a program needn't handle non-finite values.
Results may differ from a plain program's by a relative error of at most 0.00021.
Values sent between devices are 32-bit elements; how exact they have to be, the bound alone decides.
No kernel may reach another device: no remote copies, remote signals or barrier semaphores. Data moves between devices by JAX's collectives and lax.ppermute only.
A program may use at most 64 MiB of HBM per device.

v0:
```python
import math
import jax
import jax.numpy as jnp
from jax import lax
from jax.sharding import PartitionSpec as P

RHO = 0.9
VAR_DIFF = 1.0
SQRT_THREE = 1.7320508075688772


def matern(rows, cols):
    inner = jnp.einsum("fr,fc->rc", rows, cols, precision=lax.Precision.HIGHEST)
    square = jnp.sum(rows * rows, 0)[:, None] + jnp.sum(cols * cols, 0)[None, :] - 2.0 * inner
    dist = jnp.sqrt(jnp.maximum(square, 0.0))
    return (1.0 + SQRT_THREE * dist) * jnp.exp(-SQRT_THREE * dist)


def partial_product(rows, cols, weights):
    tile = matern(rows, cols)
    return jnp.einsum("pc,rc->pr", weights, tile, precision=lax.Precision.HIGHEST)


def apply_blocked(rows, cols, weights):
    count = cols.shape[1]
    step = math.gcd(count, 2048)
    blocks = count // step
    cols_split = cols.reshape(cols.shape[0], blocks, step).transpose(1, 0, 2)
    weights_split = weights.reshape(weights.shape[0], blocks, step).transpose(1, 0, 2)

    def one_block(total, item):
        return (total + partial_product(rows, item[0], item[1]), None)

    start = jnp.zeros((weights.shape[0], rows.shape[1]), jnp.float32)
    total, _ = lax.scan(one_block, start, (cols_split, weights_split))
    return total


def per_device(low_sites, low_probes, high_probes, nested, inv_len_low, inv_len_diff):
    rows_dev = low_sites.shape[1]
    feats_block, lowp_block, highp_block = (
        lax.all_gather(low_sites, "grp", axis=1, tiled=True),
        lax.all_gather(low_probes, "grp", axis=1, tiled=True),
        lax.all_gather(high_probes, "grp", axis=1, tiled=True),
    )
    nest_block = lax.all_gather(nested, "grp", axis=0, tiled=True)
    width = feats_block.shape[1]
    base = lax.axis_index("blk") * width
    place_block = nest_block - base
    own_place = nested - base
    slots = lax.broadcasted_iota(jnp.int32, (width,), 0)
    pick_own = (slots[:, None] == own_place[None, :]).astype(jnp.float32)
    high_feats = jnp.dot(
        feats_block, pick_own, precision=lax.Precision.HIGHEST, preferred_element_type=jnp.float32
    )
    rows_low = low_sites * inv_len_low[:, None]
    rows_diff = high_feats * inv_len_diff[:, None]
    own_slots = lax.axis_index("grp") * rows_dev + lax.broadcasted_iota(jnp.int32, (rows_dev,), 0)
    spread_own = (place_block[:, None] == own_slots[None, :]).astype(jnp.float32)
    mixed_own = low_probes + RHO * jnp.dot(
        highp_block, spread_own, precision=lax.Precision.HIGHEST, preferred_element_type=jnp.float32
    )
    cols_feat = lax.all_gather(low_sites, ("blk", "grp"), axis=1, tiled=True)
    cols_weight = lax.all_gather(mixed_own, ("blk", "grp"), axis=1, tiled=True)
    cols_high = lax.all_gather(high_feats, ("blk", "grp"), axis=1, tiled=True)
    cols_hprobe = lax.all_gather(high_probes, ("blk", "grp"), axis=1, tiled=True)
    low_cols = cols_feat * inv_len_low[:, None]
    new_low = apply_blocked(rows_low, low_cols, cols_weight)
    new_diff = VAR_DIFF * apply_blocked(rows_diff, cols_high * inv_len_diff[:, None], cols_hprobe)
    low_block = lax.all_gather(new_low, "grp", axis=1, tiled=True)
    high_part = jnp.dot(
        low_block, pick_own, precision=lax.Precision.HIGHEST, preferred_element_type=jnp.float32
    )
    high_out = RHO * high_part + new_diff
    return (new_low, high_out)


def solution(mesh):
    return jax.shard_map(
        per_device,
        mesh=mesh,
        in_specs=(
            P(None, ("blk", "grp")),
            P(None, ("blk", "grp")),
            P(None, ("blk", "grp")),
            P(("blk", "grp")),
            P(),
            P(),
        ),
        out_specs=(P(None, ("blk", "grp")), P(None, ("blk", "grp"))),
        check_vma=False,
    )
```

profile of v0, /device:TPU:128, one launch (start us, length us, event | category | flops | bytes accessed | tf_op | source)
XLA Modules:
  0.0 1467.7 jit_solution(3234751607387825071)
XLA Ops:
  8.0 34.4 %all-gather = f32[8,64,8]{1,2,0:T(8,128)S(1)} all-gather(f32[1,64,8]{1,2,0:T(8,128)S(1)} %bitcast.97), channel_id=1, replica_groups=mesh['blk'=32,'grp'=8] {'grp'}, dimensions={0}, use_global_device_ids=true | all-gather | bytes 18432 | tf_op jit(solution)/shard_map/all_gather | solution.py:44
  45.2 12.8 all-reduce
  60.2 34.3 %all_gather.30 = f32[8,1024]{1,0:T(8,128)S(1)} all-gather(f32[8,128]{1,0:T(8,128)S(1)} %copy-done), channel_id=1, replica_groups=mesh['blk'=32,'grp'=8] {'grp'}, dimensions={1}, use_global_device_ids=true | all-gather | bytes 36864 | tf_op jit(solution)/shard_map/all_gather | solution.py:42
  94.5 626.2 %all-gather.1 = f32[256,64,8]{1,2,0:T(8,128)S(1)} all-gather(f32[1,64,8]{1,2,0:T(8,128)S(1)} %bitcast.98), channel_id=1, replica_groups=mesh['blk'=32,'grp'=8] {'blk','grp'}, dimensions={0}, use_global_device_ids=true | all-gather | bytes 526336 | tf_op jit(solution)/shard_map/all_gather | solution.py:66
  721.1 627.4 %all-gather.2 = f32[256,64,8]{1,2,0:T(8,128)S(1)} all-gather(f32[1,64,8]{1,2,0:T(8,128)S(1)} %bitcast.99), channel_id=1, replica_groups=mesh['blk'=32,'grp'=8] {'blk','grp'}, dimensions={0}, use_global_device_ids=true | all-gather | bytes 526336 | tf_op jit(solution)/shard_map/all_gather | solution.py:65
  1350.7 12.1 while.27
  1364.2 61.5 %while.26 = (s32[]{:T(128)}, f32[8,128]{1,0:T(8,128)S(1)}, f32[16,8,2048]{2,1,0:T(8,128)}, f32[128]{0:T(128)S(1)}, f32[16,8,2048]{2,1,0:T(8,128)S(1)}, /*index=5*/f32[8,128]{1,0:T(8,128)S(1)}, s32[]{:T(128)}, s32[]{:T(128)}) while((s32[]{:T(128)}, f32[8,128]{1,0:T(8,128)S(1)}, f32[16,8,2048]{2,1,0:T(8,128)}, f32[128]{0:T(128)S(1)}, ...), condition=%wide.region_3.4_spmd.clone, body=%wide.region_1.3_spmd.clone.sunk | while | flops 52461568 | bytes 2323059 | solution.py:35
  1364.3 2.1 fusion.65
  1368.1 2.1 fusion.65
  1372.0 2.1 fusion.65
  1375.8 2.1 fusion.65
  1379.6 2.1 fusion.65
  1383.5 2.1 fusion.65
  1387.3 2.1 fusion.65
  1391.2 2.1 fusion.65
  1395.0 2.1 fusion.65
  1398.8 2.1 fusion.65
  1402.7 2.1 fusion.65
  1406.5 2.1 fusion.65
  1410.4 2.1 fusion.65
  1414.2 2.1 fusion.65
  1418.1 2.1 fusion.65
  1421.9 2.1 fusion.65
  1425.7 34.3 %all_gather.28 = f32[8,1024]{1,0:T(8,128)S(1)} all-gather(f32[8,128]{1,0:T(8,128)S(1)} %get-tuple-element.132), channel_id=1, replica_groups=mesh['blk'=32,'grp'=8] {'grp'}, dimensions={1}, use_global_device_ids=true | all-gather | bytes 36864 | tf_op jit(solution)/shard_map/all_gather | solution.py:70
  (108 shorter events, 48.5 us)
Async XLA Ops:
  7.2 0.8 copy-start.1
  7.2 1355.6 %all-gather.8.cloned.1.call-start = ((), (), s32[]{:S(2)}) async-start(), calls=%async_computation.1 | async-start | bytes 1052672 | tf_op jit(solution)/shard_map/all_gather | solution.py:63
  7.9 1356.3 %all-gather.6.cloned.1.call-start = ((), (), s32[]{:S(2)}) async-start(), calls=%async_computation | async-start | bytes 1052672 | tf_op jit(solution)/shard_map/all_gather | solution.py:64
  42.4 0.7 copy-start.7
  44.3 0.7 copy-start.6
  57.9 0.7 copy-start.5
  59.5 0.7 copy-start
  94.5 626.2 %copy-start.4 = (f32[8]{0:T(128)S(1)}, f32[8]{0:T(128)}, u32[]{:S(2)}) copy-start(f32[8]{0:T(128)} %param.14) | copy-start | bytes 100
  1348.7 0.7 copy-start.3
  1425.7 34.3 %copy-start.2 = (f32[8,128]{1,0:T(8,128)}, f32[8,128]{1,0:T(8,128)S(1)}, u32[]{:S(2)}) copy-start(f32[8,128]{1,0:T(8,128)S(1)} %get-tuple-element.132) | copy-start | bytes 12292
Sparse Core Ops, SparseCore 0:
  9.8 546.0 all-gather.7
  558.2 541.7 all-gather.5
where the time goes:
time: 1470 us
  blocking collectives  1370 us (93%)
  matrix products  73 us (5%)
  between operations  14.8 us (1%)
    all_gather x1, blocking collectives, per_device(): cols_high = lax.all_gather(high_feats, ('blk', 'grp'), axis=1, tiled=True)  627 us
    all_gather x1, blocking collectives, per_device(): lax.all_gather(high_probes, ('blk', 'grp'), axis=1, tiled=True)  626 us
    dot_general x24, matrix products, matern(): inner = jnp.einsum('fr,fc->rc', rows, cols, precision=lax.Precision.HIGHEST)  40.2 us
    all_gather x1, blocking collectives, per_device(): lax.all_gather(high_probes, 'grp', axis=1, tiled=True)  34.4 us
    all_gather x1, blocking collectives, per_device(): low_block = lax.all_gather(new_low, 'grp', axis=1, tiled=True)  34.3 us
    all_gather x1, blocking collectives, per_device(): lax.all_gather(low_sites, 'grp', axis=1, tiled=True)  34.3 us
    dot_general x24, matrix products, partial_product(): jnp.einsum('pc,rc->pr', weights, tile, precision=lax.Precision.HIGHEST)  30.7 us
  transfers between devices with their start and end apart: 2, of which 0 were waited for; matrix products, arithmetic and copies ran while one was open for 1% of the time, Pallas kernels for 0%

commit v1 on v0

--- a/solution.py
+++ b/solution.py
@@ -62,7 +62,10 @@
     )
     cols_feat = lax.all_gather(low_sites, ("blk", "grp"), axis=1, tiled=True)
     cols_weight = lax.all_gather(mixed_own, ("blk", "grp"), axis=1, tiled=True)
-    cols_high = lax.all_gather(high_feats, ("blk", "grp"), axis=1, tiled=True)
+    devices = lax.axis_size(("blk", "grp"))
+    shards = jnp.stack([high_feats for _ in range(devices)])
+    shards = lax.all_to_all(shards, ("blk", "grp"), split_axis=0, concat_axis=0)
+    cols_high = jnp.concatenate(shards, axis=1)
     cols_hprobe = lax.all_gather(high_probes, ("blk", "grp"), axis=1, tiled=True)
     low_cols = cols_feat * inv_len_low[:, None]
     new_low = apply_blocked(rows_low, low_cols, cols_weight)

time: 1470 us -> 1200 us (0.82)
  blocking collectives: 1370 us -> 744 us
  waiting for transfers between devices: 0.74 us -> 339 us
    all_gather x1 -> x0, blocking collectives: 627 us -> none  [per_device(): cols_high = lax.all_gather(high_feats, ('blk', 'grp'), axis=1, tiled=True)]
    all_gather x1, waiting for transfers between devices: 0.02 us -> 338 us  [per_device(): cols_weight = lax.all_gather(mixed_own, ('blk', 'grp'), axis=1, tiled=True)]
  transfers between devices with their start and end apart: 2 -> 3, of which waited for: 0 -> 1; matrix products, arithmetic and copies ran while one was open for 1% -> 2% of each run, Pallas kernels for 0% -> 0%
where the time goes in v1:
time: 1200 us
  blocking collectives  744 us (62%)
  waiting for transfers between devices  339 us (28%)
  matrix products  73 us (6%)
  between operations  14.9 us (1%)
  starting transfers between devices  13.6 us (1%)
    all_gather x1, blocking collectives, per_device(): lax.all_gather(high_probes, ('blk', 'grp'), axis=1, tiled=True)  628 us
    all_gather x1, waiting for transfers between devices, per_device(): cols_weight = lax.all_gather(mixed_own, ('blk', 'grp'), axis=1, tiled=True)  338 us
    dot_general x24, matrix products, matern(): inner = jnp.einsum('fr,fc->rc', rows, cols, precision=lax.Precision.HIGHEST)  40.2 us
    all_gather x1, blocking collectives, per_device(): lax.all_gather(low_sites, 'grp', axis=1, tiled=True)  34.5 us
    all_gather x1, blocking collectives, per_device(): lax.all_gather(high_probes, 'grp', axis=1, tiled=True)  34.4 us
    all_gather x1, blocking collectives, per_device(): low_block = lax.all_gather(new_low, 'grp', axis=1, tiled=True)  34.3 us
    dot_general x24, matrix products, partial_product(): jnp.einsum('pc,rc->pr', weights, tile, precision=lax.Precision.HIGHEST)  30.7 us
  transfers between devices with their start and end apart: 3, of which 1 were waited for; matrix products, arithmetic and copies ran while one was open for 2% of the time, Pallas kernels for 0%

profile of v1, /device:TPU:128, one launch (start us, length us, event | category | flops | bytes accessed | tf_op | source)
XLA Modules:
  0.0 1197.8 jit_solution(416046895081307881)
XLA Ops:
  8.6 34.5 %all_gather.27 = f32[8,1024]{1,0:T(8,128)S(1)} all-gather(f32[8,128]{1,0:T(8,128)S(1)} %copy-done), channel_id=1, replica_groups=mesh['blk'=32,'grp'=8] {'grp'}, dimensions={1}, use_global_device_ids=true | all-gather | bytes 36864 | tf_op jit(solution)/shard_map/all_gather | solution.py:42
  45.6 13.5 %all-to-all-start = ((f32[256,1,512]{2,1,0:T(1,128)}), f32[256,1,512]{2,1,0:T(1,128)S(1)}, u32[]{:S(2)}, u32[]{:S(2)}) async-start(f32[256,1,512]{2,1,0:T(1,128)} %reshape.54), calls=%async_computation | async-start | bytes 1048576 | tf_op jit(solution)/shard_map/all_to_all | solution.py:67
  59.1 34.4 %all-gather = f32[8,64,8]{1,2,0:T(8,128)S(1)} all-gather(f32[1,64,8]{1,2,0:T(8,128)S(1)} %bitcast.93), channel_id=1, replica_groups=mesh['blk'=32,'grp'=8] {'grp'}, dimensions={0}, use_global_device_ids=true | all-gather | bytes 18432 | tf_op jit(solution)/shard_map/all_gather | solution.py:44
  95.8 12.6 %all-reduce = s32[512]{0:T(512)S(1)} all-reduce(s32[512]{0:T(512)S(1)} %dynamic-update-slice), channel_id=1, replica_groups=mesh['blk'=32,'grp'=8] {'grp'}, use_global_device_ids=true, to_apply=%add | all-reduce | flops 512 | bytes 4096
  110.0 628.1 %all-gather.1 = f32[256,64,8]{1,2,0:T(8,128)S(1)} all-gather(f32[1,64,8]{1,2,0:T(8,128)S(1)} %bitcast.94), channel_id=1, replica_groups=mesh['blk'=32,'grp'=8] {'blk','grp'}, dimensions={0}, use_global_device_ids=true | all-gather | bytes 526336 | tf_op jit(solution)/shard_map/all_gather | solution.py:69
  742.8 12.1 %while.27 = (s32[]{:T(128)}, f32[8,64]{1,0:T(8,128)S(1)}, f32[8,8,2048]{2,0,1:T(8,128)S(1)}, f32[64]{0:T(128)S(1)}, f32[8,8,2048]{2,0,1:T(8,128)S(1)}, /*index=5*/f32[8,64]{1,0:T(8,128)S(1)}, s32[]{:T(128)}, s32[]{:T(128)}) while((s32[]{:T(128)}, f32[8,64]{1,0:T(8,128)S(1)}, f32[8,8,2048]{2,0,1:T(8,128)S(1)}, f32[64]{0:T(128)S(1)}, ...), condition=%wide.region_7.8_spmd.clone, body=%wide.region_5.0_spmd.clone.sunk | while | flops 26246148 | bytes 1530219 | solution.py:35
  756.3 338.1 %all-gather.5.cloned.1.call-done = f32[8,32768]{1,0:T(8,128)} async-done(((f32[8,128]{1,0:T(8,128)}), f32[8,32768]{1,0:T(8,128)}) %all-gather.5.cloned.1.call-update) | async-done | bytes 1048592 | tf_op jit(solution)/shard_map/all_gather | solution.py:64
  1094.4 61.4 %while.26 = (s32[]{:T(128)}, f32[8,128]{1,0:T(8,128)S(1)}, f32[16,8,2048]{2,1,0:T(8,128)}, f32[128]{0:T(128)S(1)}, f32[16,8,2048]{2,1,0:T(8,128)S(1)}, /*index=5*/f32[8,128]{1,0:T(8,128)S(1)}, s32[]{:T(128)}, s32[]{:T(128)}) while((s32[]{:T(128)}, f32[8,128]{1,0:T(8,128)S(1)}, f32[16,8,2048]{2,1,0:T(8,128)}, f32[128]{0:T(128)S(1)}, ...), condition=%wide.region_3.4_spmd.clone, body=%wide.region_1.3_spmd.clone.sunk | while | flops 52461568 | bytes 2323059 | solution.py:35
  1094.4 2.1 fusion.64
  1098.2 2.1 fusion.64
  1102.1 2.1 fusion.64
  1105.9 2.1 fusion.64
  1109.8 2.1 fusion.64
  1113.6 2.1 fusion.64
  1117.4 2.1 fusion.64
  1121.3 2.1 fusion.64
  1125.1 2.1 fusion.64
  1129.0 2.1 fusion.64
  1132.8 2.1 fusion.64
  1136.7 2.1 fusion.64
  1140.5 2.1 fusion.64
  1144.3 2.1 fusion.64
  1148.2 2.1 fusion.64
  1155.8 34.3 %all_gather.25 = f32[8,1024]{1,0:T(8,128)S(1)} all-gather(f32[8,128]{1,0:T(8,128)S(1)} %get-tuple-element.132), channel_id=1, replica_groups=mesh['blk'=32,'grp'=8] {'grp'}, dimensions={1}, use_global_device_ids=true | all-gather | bytes 36864 | tf_op jit(solution)/shard_map/all_gather | solution.py:73
  (113 shorter events, 54.6 us)
Async XLA Ops:
  7.2 747.7 %all-gather.7.cloned.1.call-start = ((), (), s32[]{:S(2)}) async-start(), calls=%async_computation.2 | async-start | bytes 1052672 | tf_op jit(solution)/shard_map/all_gather | solution.py:63
  7.9 0.7 copy-start
  8.6 34.5 %copy-start.6 = (s32[64]{0:T(128)S(1)}, s32[64]{0:T(128)}, u32[]{:S(2)}) copy-start(s32[64]{0:T(128)} %param.13) | copy-start | bytes 772
  43.1 0.7 copy-start.4
  45.6 13.5 %copy-start.1 = (f32[8,64]{1,0:T(8,128)S(1)}, f32[8,64]{1,0:T(8,128)}, u32[]{:S(2)}) copy-start(f32[8,64]{1,0:T(8,128)} %param.12) | copy-start | bytes 6148
  45.6 693.9 %all-to-all-start = ((f32[256,1,512]{2,1,0:T(1,128)}), f32[256,1,512]{2,1,0:T(1,128)S(1)}, u32[]{:S(2)}, u32[]{:S(2)}) async-start(f32[256,1,512]{2,1,0:T(1,128)} %reshape.54), calls=%async_computation | async-start | bytes 1048576 | tf_op jit(solution)/shard_map/all_to_all | solution.py:67
  59.0 1035.3 %all-gather.5.cloned.1.call-start = ((), (), s32[]{:S(2)}) async-start(), calls=%async_computation.1 | async-start | bytes 1052672 | tf_op jit(solution)/shard_map/all_gather | solution.py:64
  93.6 0.7 copy-start.7
  108.4 0.7 copy-start.5
  738.7 0.7 copy-start.3
  1155.8 34.3 %copy-start.2 = (f32[8,128]{1,0:T(8,128)}, f32[8,128]{1,0:T(8,128)S(1)}, u32[]{:S(2)}) copy-start(f32[8,128]{1,0:T(8,128)S(1)} %get-tuple-element.132) | copy-start | bytes 12292
Sparse Core Ops, SparseCore 0:
  9.8 546.4 all-gather.6
  558.6 535.6 all-gather.4
